TPU v7x, 256 devices: a whole 4x4x8 slice. The times are simulated.
256 devices in a mesh: seq: 64 (over y, z, core), head: 4 (over x).
Axes of the slice: x: 4, y: 4, z: 8, core: 2. Of those that a mesh axis runs over, the one named last changes fastest.
Arguments:
- queries: bfloat16 [8192, 1024], P('seq', 'head'), may hold values from -6 to 6
- raw_keys: bfloat16 [8192, 1024], P('seq', 'head'), may hold values from -6 to 6
- values: bfloat16 [8192, 1024], P('seq', 'head'), may hold values from -6 to 6
- write_rate: float32 [8192, 8], P('seq', 'head'), may hold values from 0.0005 to 1
- out_weight: bfloat16 [1024, 1024], P('head'), may hold values from -0.1875 to 0.1875
- out_grad: bfloat16 [8192, 1024], P('seq', 'head'), may hold values from -6 to 6
Outputs:
- layer_out: bfloat16 [8192, 1024], P('seq', 'head')
- query_grad: bfloat16 [8192, 1024], P('seq', 'head')
- key_grad: bfloat16 [8192, 1024], P('seq', 'head')
- value_grad: bfloat16 [8192, 1024], P('seq', 'head')
- rate_grad: float32 [8192, 8], P('seq', 'head')
All inputs are finite; a program needn't handle non-finite values.
Results may differ from a plain program's by a relative error of at most 0.0049.
Values may be sent and summed in bfloat16 or wider, within the bound.
No kernel may reach another device: no remote copies, remote signals or barrier semaphores. Data moves between devices by JAX's collectives and lax.ppermute only.
A program may use at most 128 MiB of HBM per device.

v0:
```python
import jax
import jax.numpy as jnp
from jax import lax
from jax.sharding import PartitionSpec as P

BLOCK = 64
epsilon = 1e-06
highest = lax.Precision.HIGHEST


def prefix(part, axis, combine, identity, reverse):
    count = lax.axis_size(axis)
    place = lax.axis_index(axis)
    ahead = count - 1 - place if reverse else place
    gathered = jax.tree.map(lambda a: lax.all_gather(a, axis), part)
    state = jax.tree.map(lambda a, e: jnp.zeros_like(a) + jnp.asarray(e, a.dtype), part, identity)

    def one(turn, state):
        source = count - 1 - turn if reverse else turn
        return combine(
            state, jax.tree.map(lambda a: lax.dynamic_index_in_dim(a, source, 0, False), gathered)
        )

    return lax.fori_loop(0, ahead, one, state)


def unit_rows(array):
    return array * lax.rsqrt(jnp.sum(array * array, -1, keepdims=True) + epsilon)


def to_blocks(array, head_count):
    rows = array.shape[0]
    head_width = array.shape[1] // head_count
    return array.reshape(rows // BLOCK, BLOCK, head_count, head_width).transpose(2, 0, 1, 3)


def rate_blocks(decay_rate):
    rows = decay_rate.shape[0]
    head_count = decay_rate.shape[1]
    return decay_rate.reshape(rows // BLOCK, BLOCK, head_count).transpose(2, 0, 1)


def from_blocks(block_outputs):
    block_count, head_count, size, head_width = block_outputs.shape
    return block_outputs.transpose(0, 2, 1, 3).reshape(block_count * size, head_count * head_width)


def block_factors(query_blocks, key_blocks, value_blocks, rate_parts):
    unit_query = unit_rows(query_blocks)
    unit_key = unit_rows(key_blocks)
    size = unit_key.shape[-2]
    identity_block = jnp.eye(size, dtype=jnp.float32)
    key_gram = jnp.einsum(
        "hncd,hnsd->hncs", unit_key * rate_parts[..., None], unit_key, precision=highest
    )
    strict_lower = jnp.tril(key_gram, -1)
    result = identity_block - strict_lower
    power_term = strict_lower
    span_done = 2
    while span_done < size:
        power_term = jnp.einsum("hnij,hnjk->hnik", power_term, power_term, precision=highest)
        result = result + jnp.einsum("hnij,hnjk->hnik", result, power_term, precision=highest)
        span_done = span_done * 2
    scaled = result * rate_parts[..., None, :]
    key_mix = jnp.einsum("hncs,hnsd->hncd", scaled, unit_key, precision=highest)
    value_mix = jnp.einsum("hncs,hnsd->hncd", scaled, value_blocks, precision=highest)
    causal_scores = jnp.tril(jnp.einsum("hncd,hnsd->hncs", unit_query, unit_key, precision=highest))
    return (unit_query, unit_key, key_mix, value_mix, causal_scores)


def run_blocks(factors, start_state):
    moved = tuple((jnp.moveaxis(member, 1, 0) for member in factors))

    def advance_block(state, pieces):
        unit_query, unit_key, key_mix, value_mix, causal_scores = pieces
        innovation = value_mix - jnp.einsum("hcd,hde->hce", key_mix, state, precision=highest)
        block_out = jnp.einsum("hcd,hde->hce", unit_query, state, precision=highest)
        block_out = block_out + jnp.einsum(
            "hcs,hse->hce", causal_scores, innovation, precision=highest
        )
        state = state + jnp.einsum("hcd,hce->hde", unit_key, innovation, precision=highest)
        return (state, block_out)

    return lax.scan(advance_block, start_state, moved)


def compose(earlier, later):
    early_map, early_shift = earlier
    late_map, late_shift = later
    joined_map = jnp.einsum("hij,hjk->hik", late_map, early_map, precision=highest)
    joined_shift = jnp.einsum("hij,hjk->hik", late_map, early_shift, precision=highest) + late_shift
    return (joined_map, joined_shift)


def body(queries, raw_keys, values, write_rate, out_weight, out_grad):
    head_count = write_rate.shape[1]
    head_width = queries.shape[1] // head_count
    token_count = queries.shape[0]

    def factor_inputs(float_query, float_key, float_value, rates):
        return block_factors(
            to_blocks(float_query, head_count),
            to_blocks(float_key, head_count),
            to_blocks(float_value, head_count),
            rate_blocks(rates),
        )

    factors, pull_factors = jax.vjp(
        factor_inputs,
        queries.astype(jnp.float32),
        raw_keys.astype(jnp.float32),
        values.astype(jnp.float32),
        write_rate,
    )
    unit_query, unit_key, key_mix, value_mix, causal_scores = factors
    identity_heads = jnp.broadcast_to(
        jnp.eye(head_width, dtype=jnp.float32), (head_count, head_width, head_width)
    )
    zero_heads = jnp.zeros((head_count, head_width, head_width), jnp.float32)
    widened = (
        unit_query,
        unit_key,
        key_mix,
        jnp.concatenate([jnp.zeros_like(value_mix), value_mix], -1),
        causal_scores,
    )
    joined_state, joined_outputs = run_blocks(
        widened, jnp.concatenate([identity_heads, zero_heads], -1)
    )
    transition = joined_state[..., :head_width]
    offset = joined_state[..., head_width:]
    query_effect = joined_outputs[..., :head_width]
    attended_grad = lax.dot_general(
        lax.all_gather(out_grad, "head", axis=1, tiled=True),
        out_weight,
        (((1,), (1,)), ((), ())),
        preferred_element_type=jnp.float32,
    )
    grad_blocks = attended_grad.reshape(
        token_count // BLOCK, BLOCK, head_count, head_width
    ).transpose(0, 2, 1, 3)
    local_adjoint = jnp.einsum("nhcd,nhce->hde", query_effect, grad_blocks, precision=highest)
    unused_map, entry_state = prefix(
        (transition, offset), "seq", compose, (identity_heads, zero_heads), False
    )
    unused_adjoint_map, exit_adjoint = prefix(
        (jnp.swapaxes(transition, 1, 2), local_adjoint),
        "seq",
        compose,
        (identity_heads, zero_heads),
        True,
    )

    def run_from_entry(factor_tuple):
        return run_blocks(factor_tuple, entry_state)

    (final_state, block_outputs), pull_run = jax.vjp(run_from_entry, factors)
    factor_grads = pull_run((exit_adjoint, grad_blocks))
    query_part, key_part, value_part, rate_grad = pull_factors(factor_grads[0])
    attended_bf = from_blocks(block_outputs).astype(jnp.bfloat16)
    partial_out = jnp.dot(attended_bf, out_weight, preferred_element_type=jnp.float32)
    layer_out = lax.psum_scatter(partial_out, "head", scatter_dimension=1, tiled=True).astype(
        jnp.bfloat16
    )
    return (
        layer_out,
        query_part.astype(jnp.bfloat16),
        key_part.astype(jnp.bfloat16),
        value_part.astype(jnp.bfloat16),
        rate_grad,
    )


def solution(mesh):
    placed = (
        P("seq", "head"),
        P("seq", "head"),
        P("seq", "head"),
        P("seq", "head"),
        P("head", None),
        P("seq", "head"),
    )
    return jax.shard_map(
        body,
        mesh=mesh,
        in_specs=placed,
        out_specs=(
            P("seq", "head"),
            P("seq", "head"),
            P("seq", "head"),
            P("seq", "head"),
            P("seq", "head"),
        ),
        check_vma=False,
    )
```

profile of v0, /device:TPU:8, one launch (start us, length us, event | category | flops | bytes accessed | tf_op | source)
XLA Modules:
  0.0 506.4 jit_solution(13383869806528043871)
XLA Ops:
  16.5 4.0 while.78
  20.5 12.6 %all_gather.33 = bf16[128,1024]{1,0:T(8,128)(2,1)S(1)} all-gather(bf16[128,256]{1,0:T(8,128)(2,1)S(1)} %copy-done.15), channel_id=1, replica_groups=mesh['seq'=64,'head'=4] {'head'}, dimensions={1}, use_global_device_ids=true | all-gather | bytes 327680 | tf_op jit(solution)/shard_map/all_gather | solution.py:134
  33.5 1.9 convolution_bitcast_fusion.4
  39.1 80.6 %all-gather.15.cloned.1.call-done = f32[128,128,128]{2,1,0:T(8,128)} async-done(((f32[2,128,128]{2,1,0:T(8,128)}), f32[128,128,128]{2,1,0:T(8,128)}) %all-gather.15.cloned.1.call-update) | async-done | bytes 8388624 | tf_op jit(solution)/shard_map/all_gather | solution.py:15
  119.6 82.6 %all-gather.13.cloned.1.call-done = f32[128,128,128]{2,1,0:T(8,128)} async-done(((f32[2,128,128]{2,1,0:T(8,128)}), f32[128,128,128]{2,1,0:T(8,128)}) %all-gather.13.cloned.1.call-update) | async-done | bytes 8388624 | tf_op jit(solution)/shard_map/all_gather | solution.py:15
  202.2 60.8 %while.81 = (s32[]{:T(128)}, f32[2,128,128]{2,1,0:T(8,128)S(1)}, s32[]{:T(128)}, f32[64,2,128,128]{3,2,1,0:T(8,128)}, f32[64,2,128,128]{3,2,1,0:T(8,128)}, /*index=5*/s32[]{:T(128)}, s32[]{:T(128)}, s32[]{:T(128)}, s32[]{:T(128)}) while((s32[]{:T(128)}, f32[2,128,128]{2,1,0:T(8,128)S(1)}, s32[]{:T(128)}, f32[64,2,128,128]{3,2,1,0:T(8,128)}, ...), condition=%wide.region_10.11_spmd, body=%wide.region_9.10_spmd.sunk | while | flops 50364420 | bytes 787595 | solution.py:24
  202.3 1.2 convolution_add_fusion.38
  203.6 1.2 convolution_add_fusion.38
  204.9 1.2 convolution_add_fusion.38
  206.2 1.2 convolution_add_fusion.38
  207.4 1.2 convolution_add_fusion.38
  208.7 1.2 convolution_add_fusion.38
  210.0 1.2 convolution_add_fusion.38
  211.3 1.2 convolution_add_fusion.38
  212.6 1.2 convolution_add_fusion.38
  213.9 1.2 convolution_add_fusion.38
  215.2 1.3 convolution_add_fusion.38
  216.5 1.2 convolution_add_fusion.38
  217.8 1.2 convolution_add_fusion.38
  219.1 1.2 convolution_add_fusion.38
  220.4 1.2 convolution_add_fusion.38
  221.7 1.2 convolution_add_fusion.38
  223.0 1.2 convolution_add_fusion.38
  224.3 1.2 convolution_add_fusion.38
  225.6 1.2 convolution_add_fusion.38
  226.8 1.2 convolution_add_fusion.38
  228.1 1.2 convolution_add_fusion.38
  229.4 1.2 convolution_add_fusion.38
  230.7 1.2 convolution_add_fusion.38
  232.0 1.2 convolution_add_fusion.38
  233.3 1.2 convolution_add_fusion.38
  234.6 1.2 convolution_add_fusion.38
  235.9 1.2 convolution_add_fusion.38
  237.2 1.2 convolution_add_fusion.38
  238.5 1.2 convolution_add_fusion.38
  239.8 1.2 convolution_add_fusion.38
  241.1 1.2 convolution_add_fusion.38
  242.4 1.2 convolution_add_fusion.38
  243.6 1.2 convolution_add_fusion.38
  244.9 1.2 convolution_add_fusion.38
  246.2 1.2 convolution_add_fusion.38
  247.5 1.2 convolution_add_fusion.38
  248.8 1.2 convolution_add_fusion.38
  250.1 1.2 convolution_add_fusion.38
  251.4 1.2 convolution_add_fusion.38
  252.7 1.2 convolution_add_fusion.38
  254.0 1.2 convolution_add_fusion.38
  255.3 1.2 convolution_add_fusion.38
  256.6 1.2 convolution_add_fusion.38
  257.9 1.3 convolution_add_fusion.38
  259.2 1.3 convolution_add_fusion.38
  260.5 1.2 convolution_add_fusion.38
  261.8 1.2 convolution_add_fusion.38
  263.1 21.8 %all-gather.9.cloned.1.call-done = f32[128,128,128]{2,1,0:T(8,128)} async-done(((f32[2,128,128]{2,1,0:T(8,128)}), f32[128,128,128]{2,1,0:T(8,128)}) %all-gather.9.cloned.1.call-update) | async-done | bytes 8388624 | tf_op jit(solution)/shard_map/all_gather | solution.py:15
  284.9 82.4 %all-gather.11.cloned.1.call-done = f32[128,128,128]{2,1,0:T(8,128)} async-done(((f32[2,128,128]{2,1,0:T(8,128)}), f32[128,128,128]{2,1,0:T(8,128)}) %all-gather.11.cloned.1.call-update) | async-done | bytes 8388624 | tf_op jit(solution)/shard_map/all_gather | solution.py:15
  367.3 20.8 %while.79 = (s32[]{:T(128)}, f32[2,128,128]{2,1,0:T(8,128)S(1)}, s32[]{:T(128)}, f32[64,2,128,128]{3,2,1,0:T(8,128)}, f32[64,2,128,128]{3,2,1,0:T(8,128)}, /*index=5*/s32[]{:T(128)}, s32[]{:T(128)}, s32[]{:T(128)}) while((s32[]{:T(128)}, f32[2,128,128]{2,1,0:T(8,128)S(1)}, s32[]{:T(128)}, f32[64,2,128,128]{3,2,1,0:T(8,128)}, ...), condition=%wide.region_5.6_spmd, body=%wide.region_4.5_spmd.sunk | while | flops 50364420 | bytes 787575 | solution.py:24
  367.4 1.2 convolution_add_fusion.36
  368.6 1.2 convolution_add_fusion.36
  371.2 1.2 convolution_add_fusion.36
  373.8 1.2 convolution_add_fusion.36
  388.2 3.5 while.80
  394.3 10.4 %while.82 = (s32[]{:T(128)}, f32[2,128,128]{2,1,0:T(8,128)S(1)}, f32[2,2,64,128]{3,2,0,1:T(8,128)}, f32[2,2,64,128]{3,2,0,1:T(8,128)}, f32[2,2,64,128]{3,2,1,0:T...) while((s32[]{:T(128)}, f32[2,128,128]{2,1,0:T(8,128)S(1)}, ...), condition=%wide.region_12.13_spmd, body=%wide.region_11.12_spmd.sunk | while | flops 176275456 | bytes 2367137 | solution.py:84
  420.9 77.4 %reduce-scatter.2.cloned.1.call-done = f32[128,256]{1,0:T(8,128)} async-done(((f32[128,1024]{1,0:T(8,128)}), f32[128,256]{1,0:T(8,128)}) %reduce-scatter.2.cloned.1.call-update) | async-done | bytes 131088 | tf_op jit(solution)/shard_map/reduce_scatter | solution.py:162
  498.3 1.5 convert_element_type.51
  (258 shorter events, 64.6 us)
Async XLA Ops:
  7.2 25.9 %copy-start = (bf16[256,1024]{1,0:T(8,128)(2,1)S(1)}, bf16[256,1024]{1,0:T(8,128)(2,1)}, u32[]{:S(2)}) copy-start(bf16[256,1024]{1,0:T(8,128)(2,1)} %param.20) | copy-start | bytes 1572868
  7.2 112.4 %all-gather.15.cloned.1.call-start = ((), (), s32[]{:S(2)}) async-start(), calls=%async_computation.5 | async-start | bytes 8519680 | tf_op jit(solution)/shard_map/all_gather | solution.py:15
  7.2 4.0 copy-start.10
  8.4 3.7 copy-start.20
  9.4 2.7 copy-start.18
  10.3 0.8 copy-start.13
  10.3 4.7 copy-start.16
  11.6 1.4 copy-start.3
  12.4 8.1 %copy-start.15 = (bf16[128,256]{1,0:T(8,128)(2,1)S(1)}, bf16[128,256]{1,0:T(8,128)(2,1)}, u32[]{:S(2)}) copy-start(bf16[128,256]{1,0:T(8,128)(2,1)} %param.21) | copy-start | bytes 196612
  12.7 3.8 copy-start.1
  14.7 0.6 copy-start.9
  35.4 166.8 %all-gather.13.cloned.1.call-start = ((), (), s32[]{:S(2)}) async-start(), calls=%async_computation.4 | async-start | bytes 8519680 | tf_op jit(solution)/shard_map/all_gather | solution.py:15
  37.0 247.8 %all-gather.9.cloned.1.call-start = ((), (), s32[]{:S(2)}) async-start(), calls=%async_computation.2 | async-start | bytes 8519680 | tf_op jit(solution)/shard_map/all_gather | solution.py:15
  37.8 329.5 %all-gather.11.cloned.1.call-start = ((), (), s32[]{:S(2)}) async-start(), calls=%async_computation.3 | async-start | bytes 8519680 | tf_op jit(solution)/shard_map/all_gather | solution.py:15
  38.3 460.0 %reduce-scatter.2.cloned.1.call-start = ((), (), s32[]{:S(2)}) async-start(), calls=%async_computation.1 | async-start | bytes 655360 | tf_op jit(solution)/shard_map/reduce_scatter | solution.py:162
  392.4 17.0 %copy-start.2 = (f32[2,2,64,64]{3,2,1,0:T(8,128)S(1)}, f32[2,2,64,64]{3,2,1,0:T(8,128)}, u32[]{:S(2)}) copy-start(f32[2,2,64,64]{3,2,1,0:T(8,128)} %copy-done.1) | copy-start | bytes 196612
  394.3 17.3 %copy-start.4 = (f32[2,2,64,64]{3,2,1,0:T(8,128)S(1)}, f32[2,2,64,64]{3,2,1,0:T(8,128)}, u32[]{:S(2)}) copy-start(f32[2,2,64,64]{3,2,1,0:T(8,128)} %copy-done.3) | copy-start | bytes 196612
  404.7 8.1 %copy-start.11 = (f32[64,64]{1,0:T(8,128)S(1)}, f32[64,64]{1,0:T(8,128)}, u32[]{:S(2)}) copy-start(f32[64,64]{1,0:T(8,128)} %copy-done.10) | copy-start | bytes 49156
  404.7 9.2 %copy-start.14 = (pred[64,64]{1,0:T(8,128)(4,1)S(1)}, pred[64,64]{1,0:T(8,128)(4,1)}, u32[]{:S(2)}) copy-start(pred[64,64]{1,0:T(8,128)(4,1)} %copy-done.13) | copy-start | bytes 12292
  404.7 10.0 %copy-start.7 = (f32[2,2,64,64]{3,2,1,0:T(8,128)S(1)}, f32[2,2,64,64]{3,2,1,0:T(8,128)}, u32[]{:S(2)}) copy-start(f32[2,2,64,64]{3,2,1,0:T(8,128)} %get-tuple-element.516) | copy-start | bytes 196612
  404.7 10.0 %copy-start.17 = (f32[2,2,64]{2,1,0:T(2,128)S(1)}, f32[2,2,64]{2,1,0:T(2,128)}, u32[]{:S(2)}) copy-start(f32[2,2,64]{2,1,0:T(2,128)} %copy-done.16) | copy-start | bytes 3076
  404.7 10.5 %copy-start.6 = (f32[2,2,64,128]{3,2,0,1:T(8,128)S(1)}, f32[2,2,64,128]{3,2,0,1:T(8,128)}, u32[]{:S(2)}) copy-start(f32[2,2,64,128]{3,2,0,1:T(8,128)} %get-tuple-element.517) | copy-start | bytes 393220
  404.8 11.0 %copy-start.21 = (f32[2,2,64]{2,1,0:T(2,128)S(1)}, f32[2,2,64]{2,1,0:T(2,128)}, u32[]{:S(2)}) copy-start(f32[2,2,64]{2,1,0:T(2,128)} %copy-done.20) | copy-start | bytes 3076
  404.8 11.0 %copy-start.12 = (bf16[2,2,64,128]{3,2,1,0:T(8,128)(2,1)S(1)}, bf16[2,2,64,128]{3,2,1,0:T(8,128)(2,1)}, u32[]{:S(2)}) copy-start(bf16[2,2,64,128]{3,2,1,0:T(8,128)(2,1)} %get-tuple-element.510) | copy-start | bytes 196612
  404.8 13.7 %copy-start.8 = (f32[2,2,64,128]{3,2,1,0:T(8,128)S(1)}, f32[2,2,64,128]{3,2,1,0:T(8,128)}, u32[]{:S(2)}) copy-start(f32[2,2,64,128]{3,2,1,0:T(8,128)} %get-tuple-element.519) | copy-start | bytes 393220
  404.8 14.8 %copy-start.5 = (f32[2,2,64,128]{3,2,0,1:T(8,128)S(1)}, f32[2,2,64,128]{3,2,0,1:T(8,128)}, u32[]{:S(2)}) copy-start(f32[2,2,64,128]{3,2,0,1:T(8,128)} %get-tuple-element.515) | copy-start | bytes 393220
  404.8 15.3 %copy-start.19 = (f32[2,2,64]{2,1,0:T(2,128)S(1)}, f32[2,2,64]{2,1,0:T(2,128)}, u32[]{:S(2)}) copy-start(f32[2,2,64]{2,1,0:T(2,128)} %copy-done.18) | copy-start | bytes 3076
Sparse Core Ops, SparseCore 0:
  35.6 84.0 all-gather.14
  122.4 79.7 all-gather.12
  205.0 79.8 all-gather.8
  287.5 79.7 all-gather.10
  417.1 81.1 reduce-scatter.1
where the time goes:
time: 508 us; the launch traced here: 506 us
  waiting for transfers between devices  346 us (68%)
  matrix products  115 us (23%)
  between operations  14.6 us (3%)
  blocking collectives  12.6 us (2%)
  local copies, waits for them, and re-layouts  12 us (2%)
    all_gather x4, waiting for transfers between devices, prefix(): gathered = jax.tree.map(lambda a: lax.all_gather(a, axis), part)  267 us
    dot_general x63, matrix products, compose(): jnp.einsum('hij,hjk->hik', late_map, early_shift, precision=highest)  78.3 us
    reduce_scatter x1, waiting for transfers between devices, body(): lax.psum_scatter(partial_out, 'head', scatter_dimension=1, tiled=True)  77.4 us
    all_gather x1, blocking collectives, body(): lax.all_gather(out_grad, 'head', axis=1, tiled=True)  12.6 us
  transfers between devices with their start and end apart: 5, of which 5 were waited for; matrix products, arithmetic and copies ran while one was open for 13% of the time, Pallas kernels for 0%

commit v1 on v0

--- a/solution.py
+++ b/solution.py
@@ -6,6 +6,27 @@
 BLOCK = 64
 epsilon = 1e-06
 highest = lax.Precision.HIGHEST
+
+
+def ring_gather(x, axis, dim):
+    size, here, span = (lax.axis_size(axis), lax.axis_index(axis), x.shape[dim])
+    right = [(i, (i + 1) % size) for i in range(size)]
+    left = [(i, (i - 1) % size) for i in range(size)]
+    result = jnp.zeros((*x.shape[:dim], size * span, *x.shape[dim + 1 :]), x.dtype)
+    result = lax.dynamic_update_slice_in_dim(result, x, here * span, axis=dim)
+    from_left = from_right = x
+    half = size // 2
+    for step in range(1, half + 1):
+        from_left = lax.ppermute(from_left, axis, right)
+        result = lax.dynamic_update_slice_in_dim(
+            result, from_left, (here - step) % size * span, axis=dim
+        )
+        if step < size - half:
+            from_right = lax.ppermute(from_right, axis, left)
+            result = lax.dynamic_update_slice_in_dim(
+                result, from_right, (here + step) % size * span, axis=dim
+            )
+    return result
 
 
 def prefix(part, axis, combine, identity, reverse):
@@ -131,7 +152,7 @@
     offset = joined_state[..., head_width:]
     query_effect = joined_outputs[..., :head_width]
     attended_grad = lax.dot_general(
-        lax.all_gather(out_grad, "head", axis=1, tiled=True),
+        ring_gather(out_grad, "head", 1),
         out_weight,
         (((1,), (1,)), ((), ())),
         preferred_element_type=jnp.float32,

time: 508 us -> 475 us (0.935)
  the two profiles are of different devices: /device:TPU:8 before, /device:TPU:2 now
where the time goes in v1:
time: 475 us; the launch traced here: 473 us
  waiting for transfers between devices  321 us (68%)
  matrix products  115 us (24%)
  between operations  14.6 us (3%)
  local copies, waits for them, and re-layouts  13.3 us (3%)
    all_gather x4, waiting for transfers between devices, prefix(): gathered = jax.tree.map(lambda a: lax.all_gather(a, axis), part)  313 us
    dot_general x63, matrix products, compose(): jnp.einsum('hij,hjk->hik', late_map, early_shift, precision=highest)  78.2 us
  transfers between devices with their start and end apart: 8, of which 6 were waited for; matrix products, arithmetic and copies ran while one was open for 24% of the time, Pallas kernels for 0%

profile of v1, /device:TPU:2, one launch (start us, length us, event | category | flops | bytes accessed | tf_op | source)
XLA Modules:
  0.0 473.1 jit_solution(11798860399108995909)
XLA Ops:
  16.8 4.0 while.78
  23.2 1.6 collective-permute-start
  25.7 2.1 collective-permute-done
  27.8 1.3 collective-permute-start.2
  29.1 4.1 collective-permute-done.2
  33.6 2.0 convolution_bitcast_fusion.4
  36.3 71.3 %all-gather.9.cloned.1.call-done = f32[128,128,128]{2,1,0:T(8,128)} async-done(((f32[2,128,128]{2,1,0:T(8,128)}), f32[128,128,128]{2,1,0:T(8,128)}) %all-gather.9.cloned.1.call-update) | async-done | bytes 8388624 | tf_op jit(solution)/shard_map/all_gather | solution.py:36
  107.7 82.6 %all-gather.11.cloned.1.call-done = f32[128,128,128]{2,1,0:T(8,128)} async-done(((f32[2,128,128]{2,1,0:T(8,128)}), f32[128,128,128]{2,1,0:T(8,128)}) %all-gather.11.cloned.1.call-update) | async-done | bytes 8388624 | tf_op jit(solution)/shard_map/all_gather | solution.py:36
  190.3 3.5 while.80
  195.8 77.1 %all-gather.13.cloned.1.call-done = f32[128,128,128]{2,1,0:T(8,128)} async-done(((f32[2,128,128]{2,1,0:T(8,128)}), f32[128,128,128]{2,1,0:T(8,128)}) %all-gather.13.cloned.1.call-update) | async-done | bytes 8388624 | tf_op jit(solution)/shard_map/all_gather | solution.py:36
  272.9 82.5 %all-gather.15.cloned.1.call-done = f32[128,128,128]{2,1,0:T(8,128)} async-done(((f32[2,128,128]{2,1,0:T(8,128)}), f32[128,128,128]{2,1,0:T(8,128)}) %all-gather.15.cloned.1.call-update) | async-done | bytes 8388624 | tf_op jit(solution)/shard_map/all_gather | solution.py:36
  355.4 81.6 %while.81 = (s32[]{:T(128)}, f32[2,128,128]{2,1,0:T(8,128)S(1)}, s32[]{:T(128)}, f32[64,2,128,128]{3,2,1,0:T(8,128)}, f32[64,2,128,128]{3,2,1,0:T(8,128)}, /*index=5*/s32[]{:T(128)}, s32[]{:T(128)}, s32[]{:T(128)}, s32[]{:T(128)}) while((s32[]{:T(128)}, f32[2,128,128]{2,1,0:T(8,128)S(1)}, s32[]{:T(128)}, f32[64,2,128,128]{3,2,1,0:T(8,128)}, ...), condition=%wide.region_10.11_spmd, body=%wide.region_9.10_spmd.sunk | while | flops 50364420 | bytes 787595 | solution.py:45
  355.4 1.2 convolution_add_fusion.38
  356.7 1.2 convolution_add_fusion.38
  358.0 1.2 convolution_add_fusion.38
  359.3 1.2 convolution_add_fusion.38
  360.6 1.2 convolution_add_fusion.38
  361.9 1.2 convolution_add_fusion.38
  363.2 1.2 convolution_add_fusion.38
  364.5 1.2 convolution_add_fusion.38
  365.8 1.2 convolution_add_fusion.38
  367.1 1.2 convolution_add_fusion.38
  368.4 1.2 convolution_add_fusion.38
  369.7 1.2 convolution_add_fusion.38
  371.0 1.2 convolution_add_fusion.38
  372.2 1.2 convolution_add_fusion.38
  373.5 1.2 convolution_add_fusion.38
  374.8 1.2 convolution_add_fusion.38
  376.1 1.2 convolution_add_fusion.38
  377.4 1.2 convolution_add_fusion.38
  378.7 1.2 convolution_add_fusion.38
  380.0 1.2 convolution_add_fusion.38
  381.3 1.2 convolution_add_fusion.38
  382.6 1.2 convolution_add_fusion.38
  383.9 1.2 convolution_add_fusion.38
  385.2 1.2 convolution_add_fusion.38
  386.5 1.2 convolution_add_fusion.38
  387.7 1.2 convolution_add_fusion.38
  389.0 1.2 convolution_add_fusion.38
  390.3 1.2 convolution_add_fusion.38
  391.6 1.2 convolution_add_fusion.38
  392.9 1.2 convolution_add_fusion.38
  394.2 1.2 convolution_add_fusion.38
  395.5 1.2 convolution_add_fusion.38
  396.8 1.2 convolution_add_fusion.38
  398.1 1.2 convolution_add_fusion.38
  399.4 1.2 convolution_add_fusion.38
  400.7 1.2 convolution_add_fusion.38
  402.0 1.2 convolution_add_fusion.38
  403.2 1.2 convolution_add_fusion.38
  404.5 1.2 convolution_add_fusion.38
  405.8 1.2 convolution_add_fusion.38
  407.1 1.2 convolution_add_fusion.38
  408.4 1.2 convolution_add_fusion.38
  409.7 1.2 convolution_add_fusion.38
  412.3 1.2 convolution_add_fusion.38
  416.2 1.2 convolution_add_fusion.38
  420.0 1.2 convolution_add_fusion.38
  423.9 1.2 convolution_add_fusion.38
  427.8 1.2 convolution_add_fusion.38
  431.6 1.2 convolution_add_fusion.38
  435.5 1.2 convolution_add_fusion.38
  439.6 10.4 %while.82 = (s32[]{:T(128)}, f32[2,128,128]{2,1,0:T(8,128)S(1)}, f32[2,2,64,128]{3,2,0,1:T(8,128)}, f32[2,2,64,128]{3,2,0,1:T(8,128)}, f32[2,2,64,128]{3,2,1,0:T...) while((s32[]{:T(128)}, f32[2,128,128]{2,1,0:T(8,128)S(1)}, ...), condition=%wide.region_12.13_spmd, body=%wide.region_11.12_spmd.sunk | while | flops 176275456 | bytes 2367137 | solution.py:105
  465.0 1.5 convert_element_type.51
  (262 shorter events, 67.4 us)
Async XLA Ops:
  7.2 26.1 %copy-start = (bf16[256,1024]{1,0:T(8,128)(2,1)S(1)}, bf16[256,1024]{1,0:T(8,128)(2,1)}, u32[]{:S(2)}) copy-start(bf16[256,1024]{1,0:T(8,128)(2,1)} %param.20) | copy-start | bytes 1572868
  7.2 100.5 %all-gather.9.cloned.1.call-start = ((), (), s32[]{:S(2)}) async-start(), calls=%async_computation.2 | async-start | bytes 8519680 | tf_op jit(solution)/shard_map/all_gather | solution.py:36
  7.2 4.0 copy-start.8
  8.4 6.9 %copy-start.17 = (f32[2,2,64]{2,1,0:T(2,128)}, f32[2,2,64]{2,1,0:T(2,128)S(1)}, u32[]{:S(2)}) copy-start(f32[2,2,64]{2,1,0:T(2,128)S(1)} %fusion.98) | copy-start | bytes 3076
  9.4 5.9 %copy-start.15 = (f32[2,2,64]{2,1,0:T(2,128)}, f32[2,2,64]{2,1,0:T(2,128)S(1)}, u32[]{:S(2)}) copy-start(f32[2,2,64]{2,1,0:T(2,128)S(1)} %fusion.97) | copy-start | bytes 3076
  10.3 0.8 copy-start.10
  10.3 5.0 %copy-start.13 = (f32[2,2,64]{2,1,0:T(2,128)}, f32[2,2,64]{2,1,0:T(2,128)S(1)}, u32[]{:S(2)}) copy-start(f32[2,2,64]{2,1,0:T(2,128)S(1)} %get-tuple-element.713) | copy-start | bytes 3076
  11.6 0.7 copy-start.1
  13.8 9.4 %copy-start.12 = (bf16[128,256]{1,0:T(8,128)(2,1)S(1)}, bf16[128,256]{1,0:T(8,128)(2,1)}, u32[]{:S(2)}) copy-start(bf16[128,256]{1,0:T(8,128)(2,1)} %param.21) | copy-start | bytes 196612
  15.0 0.6 copy-start.7
  21.6 168.7 %all-gather.11.cloned.1.call-start = ((), (), s32[]{:S(2)}) async-start(), calls=%async_computation.3 | async-start | bytes 8519680 | tf_op jit(solution)/shard_map/all_gather | solution.py:36
  22.3 250.6 %all-gather.13.cloned.1.call-start = ((), (), s32[]{:S(2)}) async-start(), calls=%async_computation.4 | async-start | bytes 8519680 | tf_op jit(solution)/shard_map/all_gather | solution.py:36
  23.1 332.2 %all-gather.15.cloned.1.call-start = ((), (), s32[]{:S(2)}) async-start(), calls=%async_computation.5 | async-start | bytes 8519680 | tf_op jit(solution)/shard_map/all_gather | solution.py:36
  23.2 4.6 collective-permute-start
  24.8 4.3 collective-permute-start.1
  27.8 5.5 %collective-permute-start.2 = (bf16[128,256]{1,0:T(8,128)(2,1)S(1)}, bf16[128,256]{1,0:T(8,128)(2,1)S(1)}, u32[]{:S(2)}, u32[]{:S(2)}) collective-permute-start(bf16[128,256]{1,0:T(8,128)(2,1)S(1)} %collective-permute-done), channel_id=1, source_target_pairs={{0,1},{1,2},{2,3},{3,0},{4,5},{5,6},{6,7},{7,4},{8,9},{9,10},{10,1... | collective-permute-start | bytes 196616 | tf_op jit(solution)/shard_map/ppermute | solution.py:20
  35.6 429.4 %reduce-scatter.2.cloned.1.call-start = ((), (), s32[]{:S(2)}) async-start(), calls=%async_computation.1 | async-start | bytes 655360 | tf_op jit(solution)/shard_map/reduce_scatter | solution.py:183
  439.6 17.3 %copy-start.2 = (f32[2,2,64,64]{3,2,1,0:T(8,128)S(1)}, f32[2,2,64,64]{3,2,1,0:T(8,128)}, u32[]{:S(2)}) copy-start(f32[2,2,64,64]{3,2,1,0:T(8,128)} %copy-done.1) | copy-start | bytes 196612
  450.0 8.0 %copy-start.9 = (f32[64,64]{1,0:T(8,128)S(1)}, f32[64,64]{1,0:T(8,128)}, u32[]{:S(2)}) copy-start(f32[64,64]{1,0:T(8,128)} %copy-done.8) | copy-start | bytes 49156
  450.0 9.2 %copy-start.11 = (pred[64,64]{1,0:T(8,128)(4,1)S(1)}, pred[64,64]{1,0:T(8,128)(4,1)}, u32[]{:S(2)}) copy-start(pred[64,64]{1,0:T(8,128)(4,1)} %copy-done.10) | copy-start | bytes 12292
  450.0 10.0 %copy-start.5 = (f32[2,2,64,64]{3,2,1,0:T(8,128)S(1)}, f32[2,2,64,64]{3,2,1,0:T(8,128)}, u32[]{:S(2)}) copy-start(f32[2,2,64,64]{3,2,1,0:T(8,128)} %get-tuple-element.516) | copy-start | bytes 196612
  450.0 10.0 %copy-start.14 = (f32[2,2,64]{2,1,0:T(2,128)S(1)}, f32[2,2,64]{2,1,0:T(2,128)}, u32[]{:S(2)}) copy-start(f32[2,2,64]{2,1,0:T(2,128)} %copy-done.13) | copy-start | bytes 3076
  450.0 10.5 %copy-start.4 = (f32[2,2,64,128]{3,2,0,1:T(8,128)S(1)}, f32[2,2,64,128]{3,2,0,1:T(8,128)}, u32[]{:S(2)}) copy-start(f32[2,2,64,128]{3,2,0,1:T(8,128)} %get-tuple-element.517) | copy-start | bytes 393220
  450.0 11.0 %copy-start.18 = (f32[2,2,64]{2,1,0:T(2,128)S(1)}, f32[2,2,64]{2,1,0:T(2,128)}, u32[]{:S(2)}) copy-start(f32[2,2,64]{2,1,0:T(2,128)} %copy-done.17) | copy-start | bytes 3076
  450.1 12.5 %copy-start.6 = (f32[2,2,64,128]{3,2,1,0:T(8,128)S(1)}, f32[2,2,64,128]{3,2,1,0:T(8,128)}, u32[]{:S(2)}) copy-start(f32[2,2,64,128]{3,2,1,0:T(8,128)} %get-tuple-element.519) | copy-start | bytes 393220
  450.1 13.6 %copy-start.3 = (f32[2,2,64,128]{3,2,0,1:T(8,128)S(1)}, f32[2,2,64,128]{3,2,0,1:T(8,128)}, u32[]{:S(2)}) copy-start(f32[2,2,64,128]{3,2,0,1:T(8,128)} %get-tuple-element.515) | copy-start | bytes 393220
  450.1 14.1 %copy-start.16 = (f32[2,2,64]{2,1,0:T(2,128)S(1)}, f32[2,2,64]{2,1,0:T(2,128)}, u32[]{:S(2)}) copy-start(f32[2,2,64]{2,1,0:T(2,128)} %copy-done.15) | copy-start | bytes 3076
Sparse Core Ops, SparseCore 0:
  21.7 85.9 all-gather.8
  110.4 79.7 all-gather.10
  193.0 79.8 all-gather.12
  275.6 79.7 all-gather.14
  357.8 18.8 reduce-scatter.1
